TPU v7x, 256 devices: a whole 4x4x8 slice. The times are simulated.
256 devices in a mesh: req: 32 (over y, x, core), tp: 8 (over z).
Axes of the slice: x: 4, y: 4, z: 8, core: 2. Of those that a mesh axis runs over, the one named last changes fastest.
Arguments:
- queries: bfloat16 [2048, 4096], P('req', 'tp'), may hold values from -8 to 8
- suffix_kv: bfloat16 [2048, 2, 1024], P('req', None, 'tp'), may hold values from -6 to 6
- prefix_cache: bfloat16 [32, 2048, 2, 1024], P('req', None, None, 'tp'), may hold values from -8 to 8
- prefix_owner: int32 [4], replicated, may hold values from 0 to 31, as said below
- request_prefix: int32 [64], P('req'), may hold values from 0 to 3
- suffix_len: int32 [64], P('req'), may hold values from 1 to 32, 1728 in all
- residual: bfloat16 [2048, 4096], P('req'), may hold values from -40 to 40
- norm_gain: float32 [4096], replicated, may hold values from 0.1 to 1.9
- router: float32 [4096, 8], replicated, may hold values from -0.09375 to 0.09375
- routes: int32 [2048, 2], P('req'), may hold values from 0 to 7, all different within a row; in each aligned block of 64 rows (0 to 63, 64 to 127, ...) at most 18 rows name the same one
- w_gate: bfloat16 [32, 4096, 2048], P('req', None, 'tp'), may hold values from -0.09375 to 0.09375
- w_up: bfloat16 [32, 4096, 2048], P('req', None, 'tp'), may hold values from -0.09375 to 0.09375
- w_down: bfloat16 [32, 2048, 4096], P('req', 'tp'), may hold values from -0.0625 to 0.0625
- w_out: bfloat16 [4096, 4096], P('tp'), may hold values from -1 to 1
Outputs:
- layer_out: bfloat16 [2048, 4096], P('req', 'tp')
Inputs may be any that keep to these rules, and one draw needn't show every extreme that they name: `prefix_owner`: the 4 owners are distinct. Among the 64 token slots of one req index, no expert is named by more than 18 routes, and in some req indices one expert is named by exactly 18; the two experts of a token differ.
All inputs are finite; a program needn't handle non-finite values. No bound on the sum of `suffix_len` on one device may be relied on, other than what follows from the above.
Results may differ from a plain program's by a relative error of at most 0.017.
Values may be sent and summed in bfloat16 or wider, within the bound.
No kernel may reach another device: no remote copies, remote signals or barrier semaphores. Data moves between devices by JAX's collectives and lax.ppermute only.
A program may use at most 128 MiB of HBM per device.

v0:
```python
import math
import jax
import jax.numpy as jnp
from jax import lax
from jax.sharding import PartitionSpec as P

HEADS = 32
KVH = 8
HD = 128
EXPERTS = 8
NPFX = 4
CAP = 18


def broadcast(x, axis, root):
    mine = lax.axis_index(axis) == root
    return lax.psum(jnp.where(mine, x, jnp.zeros_like(x)), axis)


def attend_local(queries, suffix_kv, chosen, suffix_len, requests, slot_len):
    kv_local = suffix_kv.shape[2] // HD
    group_size = HEADS // KVH
    plen_local = chosen.shape[1]
    query_block = queries.reshape(requests, slot_len, kv_local, group_size, HD)
    cache_block = chosen.reshape(requests, plen_local, 2, kv_local, HD)
    suffix_block = suffix_kv.reshape(requests, slot_len, 2, kv_local, HD)
    score_scale = 1.0 / math.sqrt(HD)
    prefix_score = (
        jnp.einsum(
            "rikgd,rjkd->rkgij",
            query_block,
            cache_block[:, :, 0],
            preferred_element_type=jnp.float32,
        )
        * score_scale
    )
    suffix_score = (
        jnp.einsum(
            "rikgd,rjkd->rkgij",
            query_block,
            suffix_block[:, :, 0],
            preferred_element_type=jnp.float32,
        )
        * score_scale
    )
    positions = jnp.arange(slot_len, dtype=jnp.int32)
    allowed = (positions[None, None, :] <= positions[None, :, None]) & (
        positions[None, None, :] < suffix_len[:, None, None]
    )
    suffix_score = jnp.where(allowed[:, None, None], suffix_score, -1e30)
    score_peak = jnp.maximum(prefix_score.max(-1), suffix_score.max(-1))[..., None]
    prefix_exp = jnp.exp(prefix_score - score_peak)
    suffix_exp = jnp.exp(suffix_score - score_peak)
    normaliser = prefix_exp.sum(-1, keepdims=True) + suffix_exp.sum(-1, keepdims=True)
    prefix_prob = (prefix_exp / normaliser).astype(jnp.bfloat16)
    suffix_prob = (suffix_exp / normaliser).astype(jnp.bfloat16)
    mixed_values = jnp.einsum(
        "rkgij,rjkd->rikgd", prefix_prob, cache_block[:, :, 1], preferred_element_type=jnp.float32
    )
    mixed_values = mixed_values + jnp.einsum(
        "rkgij,rjkd->rikgd", suffix_prob, suffix_block[:, :, 1], preferred_element_type=jnp.float32
    )
    return mixed_values.reshape(requests * slot_len, kv_local * group_size * HD).astype(
        jnp.bfloat16
    )


def routing_tables(routes, live_rows, route_weight):
    expert_ids = jnp.arange(EXPERTS, dtype=jnp.int32)
    member = (routes[:, :, None] == expert_ids) & live_rows[:, None, None]
    member_int = member.astype(jnp.int32)
    flat_member = member_int.reshape(-1, EXPERTS)
    earlier = jnp.cumsum(flat_member, axis=0) - flat_member
    slot_index = jnp.sum(earlier * flat_member, axis=1).reshape(routes.shape)
    slot_hit = (slot_index[:, :, None] == jnp.arange(CAP, dtype=jnp.int32)).astype(jnp.float32)
    member_float = member.astype(jnp.float32)
    placing = (
        jnp.einsum("tke,tkc->ect", member_float, slot_hit)
        .reshape(EXPERTS * CAP, routes.shape[0])
        .astype(jnp.bfloat16)
    )
    combining = jnp.einsum(
        "tke,tkc,tk->tec", member_float, slot_hit, route_weight, precision=lax.Precision.HIGHEST
    )
    return (placing, combining.reshape(routes.shape[0], EXPERTS * CAP))


def expert_apply(arrived, w_gate, w_up, w_down):
    flat_rows = arrived.reshape(-1, arrived.shape[2])
    gate_value = jnp.dot(flat_rows, w_gate[0], preferred_element_type=jnp.float32)
    up_value = jnp.dot(flat_rows, w_up[0], preferred_element_type=jnp.float32)
    hidden_units = (jax.nn.silu(gate_value) * up_value).astype(jnp.bfloat16)
    piece_out = jnp.dot(hidden_units, w_down[0], preferred_element_type=jnp.float32).astype(
        jnp.bfloat16
    )
    return piece_out.reshape(arrived.shape[0], arrived.shape[1], piece_out.shape[1])


def send_back(parts):
    return lax.all_to_all(parts, "req", split_axis=0, concat_axis=0, tiled=True)


def per_device(
    queries,
    suffix_kv,
    prefix_cache,
    prefix_owner,
    request_prefix,
    suffix_len,
    residual,
    norm_gain,
    router,
    routes,
    w_gate,
    w_up,
    w_down,
    w_out,
):
    tp_count = lax.axis_size("tp")
    tp_index = lax.axis_index("tp")
    req_count = lax.axis_size("req")
    model_width = residual.shape[1]
    share_width = model_width // tp_count
    share_start = tp_index * share_width
    requests = request_prefix.shape[0]
    slot_len = queries.shape[0] // requests
    caches = []
    for prefix_index in range(NPFX):
        caches.append(broadcast(prefix_cache, "req", prefix_owner[prefix_index]))
    stacked = jnp.concatenate(caches, axis=0)
    chosen = jnp.take(stacked, request_prefix, axis=0)
    attended = attend_local(queries, suffix_kv, chosen, suffix_len, requests, slot_len)
    partial_value = jnp.dot(attended, w_out, preferred_element_type=jnp.float32)
    summed_attn = lax.psum(partial_value.astype(jnp.bfloat16), "tp").astype(jnp.float32)
    hidden_state = residual.astype(jnp.float32) + summed_attn
    inverse = lax.rsqrt(jnp.mean(hidden_state * hidden_state, axis=1, keepdims=True) + 1e-05)
    scaled = hidden_state * norm_gain * inverse
    logits = jnp.dot(scaled, router, precision=lax.Precision.HIGHEST)
    normed_full = scaled.astype(jnp.bfloat16)
    hidden_share = lax.dynamic_slice_in_dim(hidden_state, share_start, share_width, 1)
    route_hit = (routes[:, :, None] == jnp.arange(EXPERTS, dtype=jnp.int32)).astype(jnp.float32)
    picked_logit = jnp.sum(route_hit * logits[:, None, :], axis=2)
    first_weight = jax.nn.sigmoid(picked_logit[:, 0] - picked_logit[:, 1])
    route_weight = jnp.stack([first_weight, 1.0 - first_weight], axis=1)
    live_rows = jnp.arange(routes.shape[0], dtype=jnp.int32) % slot_len < jnp.repeat(
        suffix_len, slot_len
    )
    placing, combining = routing_tables(routes, live_rows, route_weight)
    repeats = req_count // EXPERTS
    send_rows = jnp.dot(placing, normed_full, preferred_element_type=jnp.float32).astype(
        jnp.bfloat16
    )
    outgoing = jnp.tile(send_rows.reshape(EXPERTS, CAP, model_width), (repeats, 1, 1))
    returned = send_back(
        expert_apply(
            lax.all_to_all(outgoing, "req", split_axis=0, concat_axis=0, tiled=True),
            w_gate,
            w_up,
            w_down,
        )
    )
    summed = returned.astype(jnp.float32).reshape(repeats, EXPERTS, CAP, model_width).sum(axis=0)
    mixture_full = jnp.dot(
        combining, summed.reshape(EXPERTS * CAP, model_width), precision=lax.Precision.HIGHEST
    )
    mixture_share = lax.psum_scatter(
        mixture_full.astype(jnp.bfloat16), "tp", scatter_dimension=1, tiled=True
    ).astype(jnp.float32)
    layer_out = jnp.where(live_rows[:, None], hidden_share + mixture_share, 0.0)
    return layer_out.astype(jnp.bfloat16)


def solution(mesh):
    return jax.shard_map(
        per_device,
        mesh=mesh,
        in_specs=(
            P("req", "tp"),
            P("req", None, "tp"),
            P("req", None, None, "tp"),
            P(),
            P("req"),
            P("req"),
            P("req", None),
            P(),
            P(),
            P("req", None),
            P("req", None, "tp"),
            P("req", None, "tp"),
            P("req", "tp", None),
            P("tp", None),
        ),
        out_specs=P("req", "tp"),
        check_vma=False,
    )
```

profile of v0, /device:TPU:2, one launch (start us, length us, event | category | flops | bytes accessed | tf_op | source)
XLA Modules:
  0.0 477.0 jit_solution(7301594830305967729)
XLA Ops:
  6.5 1.5 fusion.63
  10.6 3.3 broadcast_select_fusion.3
  14.0 0.6 copy-done.12
  15.7 122.6 %all-reduce.6.cloned.1.call-done = (bf16[1,2048,2,128]{3,1,2,0:T(8,128)(2,1)}, bf16[1,2048,2,128]{3,1,2,0:T(8,128)(2,1)}, bf16[1,2048,2,128]{3,1,2,0:T(8,128)(2,1)}, bf16[1,2048,2,128]{3,1,2,0:T(8,128)(2,1)}) async-done(((bf16[1,2048,2,128]{3,1,2,0:T(8,128)(2,1)}, bf16[1,2048,2,128]{3,1,2,0:T(8,128)(2,1)}, bf16[1,2048,2,128]{3,1,2,0:T(8,128)(2,1)}, bf16[1,2048,2,128]{3,1,2,0:T(8,128)(2,1)}), ...) | async-done | bytes 4194320 | tf_op jit(solution)/shard_map/psum | solution.py:17
  138.4 3.7 pad_maximum_fusion
  142.1 4.4 gather_fusion
  146.5 1.9 bitcast_select_fusion
  148.3 0.5 fusion.64
  148.9 0.4 fusion.7
  149.3 0.6 fusion.22
  150.2 1.4 copy-done.1
  151.5 1.6 convolution_convert_fusion.2
  153.8 0.6 fusion.16
  154.5 73.0 %all-reduce.4.cloned.1.call-done = bf16[64,4096]{1,0:T(8,128)(2,1)} async-done(((bf16[64,4096]{1,0:T(8,128)(2,1)}), bf16[64,4096]{1,0:T(8,128)(2,1)}) %all-reduce.4.cloned.1.call-update) | async-done | bytes 524304 | tf_op jit(solution)/shard_map/psum | solution.py:134
  227.5 2.4 convert_add_fusion
  229.9 1.6 convolution_convert_fusion.1
  231.5 1.3 tile.10
  232.8 2.2 tile.11
  235.0 79.5 %all_to_all.10 = bf16[32,18,4096]{2,1,0:T(8,128)(2,1)} all-to-all(bf16[32,18,4096]{2,1,0:T(8,128)(2,1)S(1)} %bitcast.105), channel_id=1, replica_groups=mesh['req'=32,'tp'=8] {'req'}, dimensions={0} | all-to-all | bytes 9437184 | tf_op jit(solution)/shard_map/all_to_all | solution.py:156
  314.5 7.7 %reshape.205 = bf16[576,4096]{1,0:T(8,128)(2,1)} reshape(bf16[32,18,4096]{2,1,0:T(8,128)(2,1)} %all_to_all.10) | data formatting | bytes 9437184 | tf_op jit(solution)/shard_map/reshape | solution.py:89
  322.2 4.4 fusion.5
  326.6 10.2 %convolution_convert_fusion = bf16[576,4096]{1,0:T(8,128)(2,1)} fusion(bf16[1,256,4096]{2,1,0:T(8,128)(2,1)S(1)} %copy-done, bf16[576,4096]{1,0:T(8,128)(2,1)} %reshape.205, bf16[1,4096,256]{2,1,0:T(8,128)(2,1)} %param.25, f32[576,256]{1,0:T(8,128)S(1)} %fusion.5), kind=kOutput, calls=%fused_computation.2 | convolution fusion | flops 2419163136 | bytes 14221312 | tf_op jit(solution)/shard_map/dot_general | solution.py:93
  336.8 7.5 %reshape.206 = bf16[32,18,4096]{2,1,0:T(8,128)(2,1)} reshape(bf16[576,4096]{1,0:T(8,128)(2,1)} %convolution_convert_fusion) | data formatting | bytes 9437184 | tf_op jit(solution)/shard_map/reshape | solution.py:96
  344.4 6.1 %all-to-all-start.1 = ((bf16[32,18,4096]{2,1,0:T(8,128)(2,1)}), bf16[32,18,4096]{2,1,0:T(8,128)(2,1)}, u32[]{:S(2)}, u32[]{:S(2)}) async-start(bf16[32,18,4096]{2,1,0:T(8,128)(2,1)} %reshape.206), calls=%async_computation.1 | async-start | bytes 12582912 | tf_op jit(solution)/shard_map/all_to_all | solution.py:100
  350.5 0.3 reduce-scatter.2.cloned.1.call-start
  350.8 1.1 fusion.25
  352.4 0.7 fusion.40
  353.2 72.6 %all-to-all-done.1 = bf16[32,18,4096]{2,1,0:T(8,128)(2,1)} async-done(((bf16[32,18,4096]{2,1,0:T(8,128)(2,1)}), bf16[32,18,4096]{2,1,0:T(8,128)(2,1)}, u32[]{:S(2)}, u32[]{:S(2)}) %all-to-all-start.1) | async-done | bytes 4718624 | tf_op jit(solution)/shard_map/all_to_all | solution.py:100
  425.8 4.3 convert_reduce_fusion
  430.1 4.2 fusion
  434.3 34.5 %reduce-scatter.2.cloned.1.call-done = bf16[64,512]{1,0:T(8,128)(2,1)} async-done(((bf16[64,4096]{1,0:T(8,128)(2,1)}), bf16[64,512]{1,0:T(8,128)(2,1)}) %reduce-scatter.2.cloned.1.call-update) | async-done | bytes 65552 | tf_op jit(solution)/shard_map/reduce_scatter | solution.py:166
  468.8 1.7 select_convert_fusion
  (63 shorter events, 2.8 us)
Async XLA Ops:
  6.5 320.1 %copy-start = (bf16[1,256,4096]{2,1,0:T(8,128)(2,1)S(1)}, bf16[1,256,4096]{2,1,0:T(8,128)(2,1)}, u32[]{:S(2)}) copy-start(bf16[1,256,4096]{2,1,0:T(8,128)(2,1)} %param.26) | copy-start | bytes 6291460
  6.5 131.8 %all-reduce.6.cloned.1.call-start = ((), (), s32[]{:S(2)}) async-start(), calls=%async_computation.5 | async-start | bytes 8388608 | tf_op jit(solution)/shard_map/psum | solution.py:17
  13.9 0.7 copy-start.12
  13.9 1.1 copy-start.9
  13.9 1.3 copy-start.7
  13.9 1.3 copy-start.6
  13.9 1.4 copy-start.11
  14.0 213.5 %all-reduce.4.cloned.1.call-start = ((), (), s32[]{:S(2)}) async-start(), calls=%async_computation.3 | async-start | bytes 1048576 | tf_op jit(solution)/shard_map/psum | solution.py:134
  149.3 2.2 copy-start.1
  153.2 74.3 %copy-start.2 = (bf16[64,4096]{1,0:T(8,128)(2,1)S(1)}, bf16[64,4096]{1,0:T(8,128)(2,1)}, u32[]{:S(2)}) copy-start(bf16[64,4096]{1,0:T(8,128)(2,1)} %param.20) | copy-start | bytes 1572868
  153.2 76.7 %copy-start.8 = (f32[4096]{0:T(1024)S(1)}, f32[4096]{0:T(1024)}, u32[]{:S(2)}) copy-start(f32[4096]{0:T(1024)} %param.21) | copy-start | bytes 49156
  227.5 2.4 copy-start.4
  344.4 6.4 %copy-start.3 = (bf16[64,4096]{1,0:T(8,128)(2,1)S(1)}, bf16[64,4096]{1,0:T(8,128)(2,1)}, u32[]{:S(2)}) copy-start(bf16[64,4096]{1,0:T(8,128)(2,1)} %param.20) | copy-start | bytes 1572868
  344.4 6.4 %copy-start.5 = (bf16[64,4096]{1,0:T(8,128)(2,1)S(1)}, bf16[64,4096]{1,0:T(8,128)(2,1)}, u32[]{:S(2)}) copy-start(bf16[64,4096]{1,0:T(8,128)(2,1)} %all-reduce.4.cloned.1.call-done) | copy-start | bytes 1572868
  344.4 6.4 %copy-start.10 = (f32[4096,8]{0,1:T(8,128)S(1)}, f32[4096,8]{0,1:T(8,128)}, u32[]{:S(2)}) copy-start(f32[4096,8]{0,1:T(8,128)} %param.22) | copy-start | bytes 393220
  344.4 81.4 %all-to-all-start.1 = ((bf16[32,18,4096]{2,1,0:T(8,128)(2,1)}), bf16[32,18,4096]{2,1,0:T(8,128)(2,1)}, u32[]{:S(2)}, u32[]{:S(2)}) async-start(bf16[32,18,4096]{2,1,0:T(8,128)(2,1)} %reshape.206), calls=%async_computation.1 | async-start | bytes 12582912 | tf_op jit(solution)/shard_map/all_to_all | solution.py:100
  350.5 118.3 %reduce-scatter.2.cloned.1.call-start = ((), (), s32[]{:S(2)}) async-start(), calls=%async_computation.4 | async-start | bytes 589824 | tf_op jit(solution)/shard_map/reduce_scatter | solution.py:166
Sparse Core Ops, SparseCore 0:
  14.1 124.2 all-reduce.5
  153.3 74.1 all-reduce.3
  434.4 34.3 reduce-scatter.1
where the time goes:
time: 478 us; the launch traced here: 477 us
  waiting for transfers between devices  303 us (63%)
  blocking collectives  79.5 us (17%)
  local copies, waits for them, and re-layouts  27.9 us (6%)
  matrix products  25.9 us (5%)
  other arithmetic  18.6 us (4%)
  between operations  15.9 us (3%)
  starting transfers between devices  6.38 us (1%)
    psum x1, waiting for transfers between devices, broadcast(): return lax.psum(jnp.where(mine, x, jnp.zeros_like(x)), axis)  123 us
    all_to_all x1, blocking collectives, per_device(): lax.all_to_all(outgoing, 'req', split_axis=0, concat_axis=0, tiled=True)  79.5 us
    psum x1, waiting for transfers between devices, per_device(): lax.psum(partial_value.astype(jnp.bfloat16), 'tp').astype(jnp.float32)  73 us
    all_to_all x1, waiting for transfers between devices, send_back(): return lax.all_to_all(parts, 'req', split_axis=0, concat_axis=0, tiled=True)  72.6 us
    reduce_scatter x1, waiting for transfers between devices, per_device(): lax.psum_scatter(mixture_full.astype(jnp.bfloat16), 'tp', scatter_dimensi...  34.5 us
    dot_general x1, matrix products, expert_apply(): jnp.dot(hidden_units, w_down[0], preferred_element_type=jnp.float32)  10.2 us
  transfers between devices with their start and end apart: 4, of which 4 were waited for; matrix products, arithmetic and copies ran while one was open for 1% of the time, Pallas kernels for 0%

commit v1 on v0

--- a/solution.py
+++ b/solution.py
@@ -131,7 +131,8 @@
     chosen = jnp.take(stacked, request_prefix, axis=0)
     attended = attend_local(queries, suffix_kv, chosen, suffix_len, requests, slot_len)
     partial_value = jnp.dot(attended, w_out, preferred_element_type=jnp.float32)
-    summed_attn = lax.psum(partial_value.astype(jnp.bfloat16), "tp").astype(jnp.float32)
+    orders_write = lambda vals, ax_name: jnp.sum(jax.lax.all_gather(vals, ax_name), axis=0)
+    summed_attn = orders_write(partial_value.astype(jnp.bfloat16), "tp").astype(jnp.float32)
     hidden_state = residual.astype(jnp.float32) + summed_attn
     inverse = lax.rsqrt(jnp.mean(hidden_state * hidden_state, axis=1, keepdims=True) + 1e-05)
     scaled = hidden_state * norm_gain * inverse

time: 478 us -> 463 us (0.969)
  waiting for transfers between devices: 303 us -> 284 us
    psum x1 -> x0, waiting for transfers between devices: 73 us -> none  [per_device(): lax.psum(partial_value.astype(jnp.bfloat16), 'tp').astype(jnp.float32)]
    all_gather x0 -> x1, waiting for transfers between devices: none -> 53.3 us  [per_device(): jax.lax.all_gather(vals, ax_name)]
where the time goes in v1:
time: 463 us; the launch traced here: 462 us
  waiting for transfers between devices  284 us (61%)
  blocking collectives  79.5 us (17%)
  local copies, waits for them, and re-layouts  29.2 us (6%)
  matrix products  26.7 us (6%)
  other arithmetic  20.6 us (4%)
  between operations  15.9 us (3%)
  starting transfers between devices  6.38 us (1%)
    psum x1, waiting for transfers between devices, broadcast(): return lax.psum(jnp.where(mine, x, jnp.zeros_like(x)), axis)  123 us
    all_to_all x1, blocking collectives, per_device(): lax.all_to_all(outgoing, 'req', split_axis=0, concat_axis=0, tiled=True)  79.5 us
    all_to_all x1, waiting for transfers between devices, send_back(): return lax.all_to_all(parts, 'req', split_axis=0, concat_axis=0, tiled=True)  72.6 us
    all_gather x1, waiting for transfers between devices, per_device(): jax.lax.all_gather(vals, ax_name)  53.3 us
    reduce_scatter x1, waiting for transfers between devices, per_device(): lax.psum_scatter(mixture_full.astype(jnp.bfloat16), 'tp', scatter_dimensi...  34.7 us
    dot_general x1, matrix products, expert_apply(): jnp.dot(hidden_units, w_down[0], preferred_element_type=jnp.float32)  10.2 us
  transfers between devices with their start and end apart: 4, of which 4 were waited for; matrix products, arithmetic and copies ran while one was open for 1% of the time, Pallas kernels for 0%

profile of v1, /device:TPU:2, one launch (start us, length us, event | category | flops | bytes accessed | tf_op | source)
XLA Modules:
  0.0 462.1 jit_solution(1291881365897656098)
XLA Ops:
  6.5 1.5 fusion.63
  10.6 3.4 broadcast_select_fusion.3
  14.0 0.7 copy-done.4
  15.3 123.1 %all-reduce.3.cloned.1.call-done = (bf16[1,2048,2,128]{3,1,2,0:T(8,128)(2,1)}, bf16[1,2048,2,128]{3,1,2,0:T(8,128)(2,1)}, bf16[1,2048,2,128]{3,1,2,0:T(8,128)(2,1)}, bf16[1,2048,2,128]{3,1,2,0:T(8,128)(2,1)}) async-done(((bf16[1,2048,2,128]{3,1,2,0:T(8,128)(2,1)}, bf16[1,2048,2,128]{3,1,2,0:T(8,128)(2,1)}, bf16[1,2048,2,128]{3,1,2,0:T(8,128)(2,1)}, bf16[1,2048,2,128]{3,1,2,0:T(8,128)(2,1)}), ...) | async-done | bytes 4194320 | tf_op jit(solution)/shard_map/psum | solution.py:17
  138.4 3.7 pad_maximum_fusion
  142.1 4.3 gather_fusion
  146.4 1.9 bitcast_select_fusion
  148.3 0.5 fusion.64
  148.9 0.4 fusion.7
  149.3 0.6 fusion.22
  150.2 1.4 copy-done.1
  151.5 1.6 convolution_convert_fusion.2
  154.4 0.6 fusion.16
  155.1 53.3 %all-gather.3.cloned.1.call-done = bf16[512,4096]{1,0:T(8,128)(2,1)} async-done(((bf16[64,4096]{1,0:T(8,128)(2,1)}), bf16[512,4096]{1,0:T(8,128)(2,1)}) %all-gather.3.cloned.1.call-update) | async-done | bytes 4194320 | tf_op jit(solution)/shard_map/all_gather | solution.py:134
  208.5 3.0 reduce_sum.68
  211.5 1.3 convert_add_fusion
  212.8 1.5 convolution_convert_fusion.1
  214.4 2.4 tile.10
  216.8 2.2 tile.11
  218.9 79.5 %all_to_all.10 = bf16[32,18,4096]{2,1,0:T(8,128)(2,1)} all-to-all(bf16[32,18,4096]{2,1,0:T(8,128)(2,1)S(1)} %bitcast.106), channel_id=1, replica_groups=mesh['req'=32,'tp'=8] {'req'}, dimensions={0} | all-to-all | bytes 9437184 | tf_op jit(solution)/shard_map/all_to_all | solution.py:157
  298.4 7.8 %reshape.205 = bf16[576,4096]{1,0:T(8,128)(2,1)} reshape(bf16[32,18,4096]{2,1,0:T(8,128)(2,1)} %all_to_all.10) | data formatting | bytes 9437184 | tf_op jit(solution)/shard_map/reshape | solution.py:89
  306.2 5.2 %fusion.5 = f32[576,256]{1,0:T(8,128)} fusion(bf16[576,4096]{1,0:T(8,128)(2,1)} %reshape.205, bf16[1,4096,256]{2,1,0:T(8,128)(2,1)} %param.24), kind=kOutput, calls=%fused_computation.13 | convolution fusion | flops 1207959552 | bytes 7405568 | tf_op jit(solution)/shard_map/dot_general | solution.py:90
  311.4 10.2 %convolution_convert_fusion = bf16[576,4096]{1,0:T(8,128)(2,1)} fusion(bf16[1,256,4096]{2,1,0:T(8,128)(2,1)S(1)} %copy-done, bf16[576,4096]{1,0:T(8,128)(2,1)} %reshape.205, bf16[1,4096,256]{2,1,0:T(8,128)(2,1)} %param.25, f32[576,256]{1,0:T(8,128)} %fusion.5), kind=kOutput, calls=%fused_computation.2 | convolution fusion | flops 2419163136 | bytes 14221312 | tf_op jit(solution)/shard_map/dot_general | solution.py:93
  321.7 7.6 %reshape.206 = bf16[32,18,4096]{2,1,0:T(8,128)(2,1)} reshape(bf16[576,4096]{1,0:T(8,128)(2,1)} %convolution_convert_fusion) | data formatting | bytes 9437184 | tf_op jit(solution)/shard_map/reshape | solution.py:96
  329.3 6.1 %all-to-all-start.1 = ((bf16[32,18,4096]{2,1,0:T(8,128)(2,1)}), bf16[32,18,4096]{2,1,0:T(8,128)(2,1)}, u32[]{:S(2)}, u32[]{:S(2)}) async-start(bf16[32,18,4096]{2,1,0:T(8,128)(2,1)} %reshape.206), calls=%async_computation.1 | async-start | bytes 12582912 | tf_op jit(solution)/shard_map/all_to_all | solution.py:100
  335.7 1.1 fusion.25
  337.3 0.7 fusion.40
  338.1 72.6 %all-to-all-done.1 = bf16[32,18,4096]{2,1,0:T(8,128)(2,1)} async-done(((bf16[32,18,4096]{2,1,0:T(8,128)(2,1)}), bf16[32,18,4096]{2,1,0:T(8,128)(2,1)}, u32[]{:S(2)}, u32[]{:S(2)}) %all-to-all-start.1) | async-done | bytes 4718624 | tf_op jit(solution)/shard_map/all_to_all | solution.py:100
  410.7 4.3 convert_reduce_fusion
  415.0 4.2 fusion
  419.2 34.7 %reduce-scatter.2.cloned.1.call-done = bf16[64,512]{1,0:T(8,128)(2,1)} async-done(((bf16[64,4096]{1,0:T(8,128)(2,1)}), bf16[64,512]{1,0:T(8,128)(2,1)}) %reduce-scatter.2.cloned.1.call-update) | async-done | bytes 65552 | tf_op jit(solution)/shard_map/reduce_scatter | solution.py:167
  453.9 1.7 select_convert_fusion
  (58 shorter events, 3.2 us)
Async XLA Ops:
  6.5 304.9 %copy-start = (bf16[1,256,4096]{2,1,0:T(8,128)(2,1)S(1)}, bf16[1,256,4096]{2,1,0:T(8,128)(2,1)}, u32[]{:S(2)}) copy-start(bf16[1,256,4096]{2,1,0:T(8,128)(2,1)} %param.26) | copy-start | bytes 6291460
  6.5 131.8 %all-reduce.3.cloned.1.call-start = ((), (), s32[]{:S(2)}) async-start(), calls=%async_computation.5 | async-start | bytes 8388608 | tf_op jit(solution)/shard_map/psum | solution.py:17
  14.0 0.8 copy-start.4
  14.0 0.9 copy-start.3
  14.0 0.9 copy-start.8
  14.0 0.9 copy-start.9
  14.0 194.5 %all-gather.3.cloned.1.call-start = ((), (), s32[]{:S(2)}) async-start(), calls=%async_computation.4 | async-start | bytes 4718592 | tf_op jit(solution)/shard_map/all_gather | solution.py:134
  149.3 2.2 copy-start.1
  151.5 2.1 copy-start.6
  208.5 3.0 copy-start.2
  211.5 1.3 copy-start.5
  329.3 6.4 %copy-start.7 = (f32[4096,8]{0,1:T(8,128)S(1)}, f32[4096,8]{0,1:T(8,128)}, u32[]{:S(2)}) copy-start(f32[4096,8]{0,1:T(8,128)} %param.22) | copy-start | bytes 393220
  329.3 81.4 %all-to-all-start.1 = ((bf16[32,18,4096]{2,1,0:T(8,128)(2,1)}), bf16[32,18,4096]{2,1,0:T(8,128)(2,1)}, u32[]{:S(2)}, u32[]{:S(2)}) async-start(bf16[32,18,4096]{2,1,0:T(8,128)(2,1)} %reshape.206), calls=%async_computation.1 | async-start | bytes 12582912 | tf_op jit(solution)/shard_map/all_to_all | solution.py:100
  335.4 118.5 %reduce-scatter.2.cloned.1.call-start = ((), (), s32[]{:S(2)}) async-start(), calls=%async_computation.3 | async-start | bytes 589824 | tf_op jit(solution)/shard_map/reduce_scatter | solution.py:167
Sparse Core Ops, SparseCore 0:
  14.1 124.2 all-reduce.2
  153.3 55.1 all-gather.2
  419.3 34.5 reduce-scatter.1
